TPU v7x, 128 devices: a whole 4x4x4 slice. The times are simulated.
128 devices in a mesh: dp: 16 (over z, y), vocab: 8 (over x, core).
Axes of the slice: x: 4, y: 4, z: 4, core: 2. Of those that a mesh axis runs over, the one named last changes fastest.
Arguments:
- hidden: bfloat16 [32, 512, 1024], P('dp'), may hold values from -24 to 24
- norm_gain: float32 [1024], replicated, may hold values from 0.5 to 1.5
- head: bfloat16 [1024, 32000], P('dp', 'vocab'), may hold values from -4 to 4
- targets: int32 [32, 512], P('dp'), may hold values from 0 to 31999
- lengths: int32 [32], P('dp'), may hold values from 1 to 512, 9216 in all
- groups: int32 [32, 1], P('dp'), may hold values from 0 to 3
- baseline: float32 [4], replicated, may hold values from -2 to 0
Outputs:
- logprob: float32 [32, 512], P('dp')
- entropy: float32 [32, 512], P('dp')
- group_shift: float32 [2, 4], replicated
Inputs may be any that keep to these rules, and one draw needn't show every extreme that they name: `groups`: every group holds at least one sequence.
All inputs are finite; a program needn't handle non-finite values. No bound on the sum of `lengths` on one device may be relied on, other than what follows from the above.
Results may differ from a plain program's by a relative error of at most 0.00045.
The roundings to bfloat16 on the way count: a program that leaves them out, or rounds other values in their place, can miss the bound.
Values may be sent and summed in bfloat16 or wider, within the bound.
No kernel may reach another device: no remote copies, remote signals or barrier semaphores. Data moves between devices by JAX's collectives and lax.ppermute only.
A program may use at most 64 MiB of HBM per device.

v0:
```python
import jax
import jax.numpy as jnp
from jax import lax
from jax.sharding import PartitionSpec as P


def per_device(hidden, norm_gain, head, targets, lengths, groups, baseline):
    seq_count, slot_count, width = hidden.shape
    total_rows = seq_count * slot_count
    block = min(512, total_rows)
    weights = lax.all_gather(head, "dp", axis=0, tiled=True)
    vocab_width = weights.shape[1]
    offset = lax.axis_index("vocab") * vocab_width
    flat = hidden.reshape(total_rows, width).astype(jnp.float32)
    square = jnp.mean(flat * flat, axis=-1, keepdims=True)
    normed = (flat * lax.rsqrt(square + 1e-05) * norm_gain[None, :]).astype(jnp.bfloat16)
    positions = jnp.arange(slot_count, dtype=jnp.int32)
    live = (positions[None, :] < lengths[:, None]).reshape(total_rows)
    wanted = targets.reshape(total_rows)
    column = jnp.arange(vocab_width, dtype=jnp.int32) + offset

    def local_stats(rows, picks):
        logits = jnp.dot(rows, weights, preferred_element_type=jnp.float32)
        local_top = jnp.max(logits, axis=-1)
        shifted = logits - local_top[:, None]
        expo = jnp.exp(shifted)
        local_total = jnp.sum(expo, axis=-1)
        local_spread = jnp.sum(expo * shifted, axis=-1)
        chosen = jnp.sum(jnp.where(column[None, :] == picks[:, None], logits, 0.0), axis=-1)
        return jnp.stack([local_top, local_total, local_spread, chosen], axis=0)

    parts = [
        local_stats(normed[start : start + block], wanted[start : start + block])
        for start in range(0, total_rows, block)
    ]
    stats = jnp.concatenate(parts, axis=1)
    vocab_count = lax.axis_size("vocab")
    spread_out = jnp.broadcast_to(stats[None], (vocab_count,) + stats.shape)
    gathered = lax.all_to_all(spread_out, "vocab", 0, 0, tiled=False)
    tops = gathered[:, 0]
    top = jnp.max(tops, axis=0)
    factor = jnp.exp(tops - top[None, :])
    total = jnp.sum(gathered[:, 1] * factor, axis=0)
    spread = jnp.sum(factor * (gathered[:, 2] + gathered[:, 1] * (tops - top[None, :])), axis=0)
    target = jnp.sum(gathered[:, 3], axis=0)
    log_total = jnp.log(total)
    logprob = target - top - log_total
    entropy = log_total - spread / total
    logprob = jnp.where(live, logprob, 0.0).reshape(seq_count, slot_count)
    entropy = jnp.where(live, entropy, 0.0).reshape(seq_count, slot_count)
    group_count = baseline.shape[0]
    member = (groups[:, 0][:, None] == jnp.arange(group_count, dtype=jnp.int32)[None, :]).astype(
        jnp.float32
    )
    seq_sums = jnp.stack(
        [jnp.sum(logprob, axis=1), jnp.sum(entropy, axis=1), lengths.astype(jnp.float32)], axis=1
    )
    partial_value = jnp.dot(member.T, seq_sums, precision=lax.Precision.HIGHEST)
    dp_count = lax.axis_size("dp")
    partial_out = jnp.broadcast_to(partial_value[None], (dp_count,) + partial_value.shape)
    group_value = jnp.sum(lax.all_to_all(partial_out, "dp", 0, 0, tiled=False), axis=0)
    group_lp, group_ent, group_cnt = (group_value[:, 0], group_value[:, 1], group_value[:, 2])
    shift = jnp.stack([group_lp / group_cnt - baseline, group_ent / group_cnt], axis=0)
    return (logprob, entropy, shift)


def solution(mesh):
    placed = (
        P("dp", None, None),
        P(),
        P("dp", "vocab"),
        P("dp", None),
        P("dp"),
        P("dp", None),
        P(),
    )
    return jax.shard_map(
        per_device,
        mesh=mesh,
        in_specs=placed,
        out_specs=(P("dp", None), P("dp", None), P()),
        check_vma=False,
    )
```

profile of v0, /device:TPU:0, one launch (start us, length us, event | category | flops | bytes accessed | tf_op | source)
XLA Modules:
  0.0 137.0 jit_solution(7105504285659255126)
XLA Ops:
  7.2 0.0 all-gather.2.cloned.1.call-start
  7.2 0.7 all-gather.2.cloned.1.call-update
  7.9 2.1 %multiply_reduce_fusion = f32[2,512]{1,0:T(2,128)S(1)} fusion(bf16[2,512,1024]{2,1,0:T(8,128)(2,1)} %param.7), kind=kLoop, calls=%fused_computation.11 | loop fusion | flops 3144704 | bytes 2101248 | tf_op jit(solution)/shard_map/reduce_sum | solution.py:15
  10.0 0.8 fusion.30
  10.8 2.1 %fusion.3 = bf16[1024,1024]{1,0:T(8,128)(2,1)S(1)} fusion(f32[1024]{0:T(1024)} %param.8, f32[1024]{0:T(1024)S(1)} %bitcast.54, bf16[2,512,1024]{2,1,0:T(8,128)(2,1)} %param.7), kind=kLoop, calls=%fused_computation.10 | loop fusion | flops 4194304 | bytes 4202496 | tf_op jit(solution)/shard_map/convert_element_type | solution.py:16
  12.9 70.6 %all-gather.2.cloned.1.call-done = bf16[1024,4000]{1,0:T(8,128)(2,1)} async-done(((bf16[64,4000]{1,0:T(8,128)(2,1)}), bf16[1024,4000]{1,0:T(8,128)(2,1)}) %all-gather.2.cloned.1.call-update) | async-done | bytes 8192016 | tf_op jit(solution)/shard_map/all_gather | solution.py:11
  83.6 7.2 %fusion.31 = (f32[512]{0:T(512)S(1)}, f32[512,4000]{0,1:T(8,128)S(1)}) fusion(bf16[1024,4000]{1,0:T(8,128)(2,1)} %all-gather.2.cloned.1.call-done, bf16[1024,1024]{1,0:T(8,128)(2,1)S(1)} %fusion.3), kind=kOutput, calls=%fused_computation.54 | convolution fusion | flops 4196351488 | bytes 17434624 | tf_op jit(solution)/shard_map/dot_general | solution.py:23
  90.8 7.2 %fusion.32 = (f32[512]{0:T(512)S(1)}, f32[512,4000]{0,1:T(8,128)S(1)}) fusion(bf16[1024,4000]{1,0:T(8,128)(2,1)} %all-gather.2.cloned.1.call-done, bf16[1024,1024]{1,0:T(8,128)(2,1)S(1)} %fusion.3), kind=kOutput, calls=%fused_computation.55 | convolution fusion | flops 4196351488 | bytes 17434624 | tf_op jit(solution)/shard_map/dot_general | solution.py:23
  97.9 0.0 copy-start
  98.0 0.0 copy-start.2
  98.0 0.0 copy-start.1
  98.0 6.6 %exponential_reduce_fusion.1 = (f32[512]{0:T(512)S(1)}, f32[512]{0:T(512)S(1)}, f32[512]{0:T(512)S(1)}, f32[512]{0:T(512)S(1)}, f32[512]{0:T(512)S(1)}, /*index=5*/f32[512]{0:T(512)S(1)}) fusion(f32[512,4000]{0,1:T(8,128)S(1)} %get-tuple-element.32, f32[512]{0:T(512)S(1)} %get-tuple-element.31, s32[512]{0:T(512)S(1)} %bitcast.63, s32[4000]{0:T(1024)S(1)} %iota_add_fusion, ...), kind=kLoop, calls=%fused_computation.3 | loop fusion | flops 28668928 | bytes 16420480 | tf_op jit(solution)/shard_map/reduce_sum | solution.py:27
  104.6 0.7 broadcast_in_dim.14
  105.2 4.3 %all-to-all-start = ((f32[8,4,1024]{2,1,0:T(4,128)}), f32[8,4,1024]{2,1,0:T(4,128)S(1)}, u32[]{:S(2)}, u32[]{:S(2)}) async-start(f32[8,4,1024]{2,1,0:T(4,128)} %broadcast_in_dim.14), calls=%async_computation | async-start | bytes 262144 | tf_op jit(solution)/shard_map/all_to_all | solution.py:39
  109.5 0.0 copy-done
  109.5 6.1 %all-to-all-done = f32[8,4,1024]{2,1,0:T(4,128)S(1)} async-done(((f32[8,4,1024]{2,1,0:T(4,128)}), f32[8,4,1024]{2,1,0:T(4,128)S(1)}, u32[]{:S(2)}, u32[]{:S(2)}) %all-to-all-start) | async-done | bytes 131104 | tf_op jit(solution)/shard_map/all_to_all | solution.py:39
  115.6 0.1 fusion.29
  115.8 0.8 fusion.27
  116.6 0.0 copy-done.2
  116.6 0.2 fusion.13
  116.8 12.7 %all_to_all.10 = f32[16,4,3]{1,2,0:T(4,128)S(1)} all-to-all(f32[16,4,3]{1,2,0:T(4,128)S(1)} %broadcast_in_dim.16), channel_id=1, replica_groups=mesh['dp'=16,'vocab'=8] {'dp'}, dimensions={0} | all-to-all | bytes 1536 | tf_op jit(solution)/shard_map/all_to_all | solution.py:61
  129.6 0.0 copy-done.1
  129.6 0.6 pad_maximum_fusion
  (13 shorter events, 0.2 us)
Async XLA Ops:
  7.2 76.4 %all-gather.2.cloned.1.call-start = ((), (), s32[]{:S(2)}) async-start(), calls=%async_computation.2 | async-start | bytes 8912896 | tf_op jit(solution)/shard_map/all_gather | solution.py:11
  97.9 11.6 %copy-start = (s32[2]{0:T(128)S(1)}, s32[2]{0:T(128)}, u32[]{:S(2)}) copy-start(s32[2]{0:T(128)} %param.11) | copy-start | bytes 28
  98.0 18.7 %copy-start.2 = (s32[2,1]{0,1:T(1,128)S(1)}, s32[2,1]{0,1:T(1,128)}, u32[]{:S(2)}) copy-start(s32[2,1]{0,1:T(1,128)} %param.12) | copy-start | bytes 28
  98.0 31.6 %copy-start.1 = (f32[4]{0:T(128)S(1)}, f32[4]{0:T(128)}, u32[]{:S(2)}) copy-start(f32[4]{0:T(128)} %param.13) | copy-start | bytes 52
  105.2 10.4 %all-to-all-start = ((f32[8,4,1024]{2,1,0:T(4,128)}), f32[8,4,1024]{2,1,0:T(4,128)S(1)}, u32[]{:S(2)}, u32[]{:S(2)}) async-start(f32[8,4,1024]{2,1,0:T(4,128)} %broadcast_in_dim.14), calls=%async_computation | async-start | bytes 262144 | tf_op jit(solution)/shard_map/all_to_all | solution.py:39
Sparse Core Ops, SparseCore 0:
  10.1 73.4 all-gather.1
where the time goes:
time: 137 us
  waiting for transfers between devices  77.4 us (56%)
  matrix products  14.5 us (11%)
  between operations  14.2 us (10%)
  blocking collectives  12.7 us (9%)
  other arithmetic  12.4 us (9%)
  starting transfers between devices  4.3 us (3%)
  local copies, waits for them, and re-layouts  1.47 us (1%)
    all_gather x1, waiting for transfers between devices, per_device(): weights = lax.all_gather(head, 'dp', axis=0, tiled=True)  70.6 us
    dot_general x2, matrix products, local_stats(): logits = jnp.dot(rows, weights, preferred_element_type=jnp.float32)  14.4 us
    all_to_all x1, blocking collectives, per_device(): lax.all_to_all(partial_out, 'dp', 0, 0, tiled=False)  12.7 us
    reduce_sum x1, other arithmetic, local_stats(): local_total = jnp.sum(expo, axis=-1)  6.58 us
    all_to_all x1, waiting for transfers between devices, per_device(): gathered = lax.all_to_all(spread_out, 'vocab', 0, 0, tiled=False)  6.09 us
    all_to_all x1, starting transfers between devices, per_device(): gathered = lax.all_to_all(spread_out, 'vocab', 0, 0, tiled=False)  4.26 us
  transfers between devices with their start and end apart: 2, of which 2 were waited for; matrix products, arithmetic and copies ran while one was open for 4% of the time, Pallas kernels for 0%

commit v1 on v0

--- a/solution.py
+++ b/solution.py
@@ -4,11 +4,29 @@
 from jax.sharding import PartitionSpec as P
 
 
+def gather_around(array, axis, dim):
+    ways, here, step = (lax.axis_size(axis), lax.axis_index(axis), array.shape[dim])
+    shape = [n * ways if d == dim else n for d, n in enumerate(array.shape)]
+    full = lax.dynamic_update_slice_in_dim(
+        jnp.zeros(shape, array.dtype), array, here * step, axis=dim
+    )
+    going_up = going_down = array
+    for far in range(1, ways // 2 + 1):
+        going_up = lax.ppermute(going_up, axis, [(d, (d + 1) % ways) for d in range(ways)])
+        full = lax.dynamic_update_slice_in_dim(full, going_up, (here - far) % ways * step, axis=dim)
+        if 2 * far < ways:
+            going_down = lax.ppermute(going_down, axis, [(d, (d - 1) % ways) for d in range(ways)])
+            full = lax.dynamic_update_slice_in_dim(
+                full, going_down, (here + far) % ways * step, axis=dim
+            )
+    return full
+
+
 def per_device(hidden, norm_gain, head, targets, lengths, groups, baseline):
     seq_count, slot_count, width = hidden.shape
     total_rows = seq_count * slot_count
     block = min(512, total_rows)
-    weights = lax.all_gather(head, "dp", axis=0, tiled=True)
+    weights = gather_around(head, "dp", 0)
     vocab_width = weights.shape[1]
     offset = lax.axis_index("vocab") * vocab_width
     flat = hidden.reshape(total_rows, width).astype(jnp.float32)

time: 137 us -> 164 us (1.20)
  starting transfers between devices: 4.3 us -> 43.1 us
  between operations: 14.2 us -> 1.17 us
  local copies, waits for them, and re-layouts: 1.47 us -> 4.18 us
  blocking collectives: 12.7 us -> 10.1 us
    ppermute x0 -> x15, waiting for transfers between devices: none -> 70.9 us  [the longest x8 70.9 us: gather_around(): lax.ppermute(going_up, axis, [(d, (d + 1) % ways) for d in range(ways)])]
    all_gather x1 -> x0, waiting for transfers between devices: 70.6 us -> none  [per_device(): weights = lax.all_gather(head, 'dp', axis=0, tiled=True)]
    ppermute x0 -> x15, starting transfers between devices: none -> 38.8 us  [the longest x7 37.1 us: gather_around(): lax.ppermute(going_down, axis, [(d, (d - 1) % ways) for d in range(ways)])]
    all_to_all x1, blocking collectives: 12.7 us -> 10.1 us  [per_device(): lax.all_to_all(partial_out, 'dp', 0, 0, tiled=False)]
    dynamic_update_slice x0 -> x16, local copies, waits for them, and re-layouts: none -> 1.67 us  [the longest x8 1.34 us: gather_around(): lax.dynamic_update_slice_in_dim(full, going_up, (here - far) % ways * ste...]
  transfers between devices with their start and end apart: 2 -> 16, of which waited for: 2 -> 9; matrix products, arithmetic and copies ran while one was open for 4% -> 5% of each run, Pallas kernels for 0% -> 0%
where the time goes in v1:
time: 164 us; the launch traced here: 163 us
  waiting for transfers between devices  77 us (47%)
  starting transfers between devices  43.1 us (26%)
  matrix products  13.8 us (8%)
  other arithmetic  13.6 us (8%)
  blocking collectives  10.1 us (6%)
  local copies, waits for them, and re-layouts  4.18 us (3%)
    ppermute x8, waiting for transfers between devices, gather_around(): lax.ppermute(going_up, axis, [(d, (d + 1) % ways) for d in range(ways)])  70.9 us
    ppermute x7, starting transfers between devices, gather_around(): lax.ppermute(going_down, axis, [(d, (d - 1) % ways) for d in range(ways)])  37.1 us
    dot_general x2, matrix products, local_stats(): logits = jnp.dot(rows, weights, preferred_element_type=jnp.float32)  13.7 us
    all_to_all x1, blocking collectives, per_device(): lax.all_to_all(partial_out, 'dp', 0, 0, tiled=False)  10.1 us
    reduce_sum x1, other arithmetic, local_stats(): local_total = jnp.sum(expo, axis=-1)  7.77 us
    all_to_all x1, waiting for transfers between devices, per_device(): gathered = lax.all_to_all(spread_out, 'vocab', 0, 0, tiled=False)  6.09 us
    all_to_all x1, starting transfers between devices, per_device(): gathered = lax.all_to_all(spread_out, 'vocab', 0, 0, tiled=False)  4.3 us
  transfers between devices with their start and end apart: 16, of which 9 were waited for; matrix products, arithmetic and copies ran while one was open for 5% of the time, Pallas kernels for 0%

profile of v1, /device:TPU:0, one launch (start us, length us, event | category | flops | bytes accessed | tf_op | source)
XLA Modules:
  0.0 163.1 jit_solution(17406810736019497409)
XLA Ops:
  0.6 0.0 copy-start
  0.6 1.8 %collective-permute-start = (bf16[64,4000]{1,0:T(8,128)(2,1)}, bf16[64,4000]{1,0:T(8,128)(2,1)}, u32[]{:S(2)}, u32[]{:S(2)}) collective-permute-start(bf16[64,4000]{1,0:T(8,128)(2,1)} %param.9), channel_id=1, source_target_pairs={{0,8},{8,16},{16,24},{24,32},{32,40},{40,48},{48,56},{56,64},{64,7... | collective-permute-start | bytes 1536008 | tf_op jit(solution)/shard_map/ppermute | solution.py:15
  2.4 5.0 %collective-permute-start.1 = (bf16[64,4000]{1,0:T(8,128)(2,1)}, bf16[64,4000]{1,0:T(8,128)(2,1)S(1)}, u32[]{:S(2)}, u32[]{:S(2)}) collective-permute-start(bf16[64,4000]{1,0:T(8,128)(2,1)} %param.9), channel_id=1, source_target_pairs={{0,120},{8,0},{16,8},{24,16},{32,24},{40,32},{48,40},{56,48},{64,5... | collective-permute-start | bytes 1536008 | tf_op jit(solution)/shard_map/ppermute | solution.py:18
  7.4 2.1 %multiply_reduce_fusion = f32[2,512]{1,0:T(2,128)S(1)} fusion(bf16[2,512,1024]{2,1,0:T(8,128)(2,1)} %param.7), kind=kLoop, calls=%fused_computation.11 | loop fusion | flops 3144704 | bytes 2101248 | tf_op jit(solution)/shard_map/reduce_sum | solution.py:33
  9.5 0.8 fusion.30
  10.3 2.1 %fusion.3 = bf16[1024,1024]{1,0:T(8,128)(2,1)S(1)} fusion(f32[1024]{0:T(1024)} %param.8, f32[1024]{0:T(1024)S(1)} %bitcast.54, bf16[2,512,1024]{2,1,0:T(8,128)(2,1)} %param.7), kind=kLoop, calls=%fused_computation.10 | loop fusion | flops 4194304 | bytes 4202496 | tf_op jit(solution)/shard_map/convert_element_type | solution.py:34
  12.7 1.0 broadcast_in_dim.15
  13.8 0.0 copy-done
  13.8 5.7 %collective-permute-done = bf16[64,4000]{1,0:T(8,128)(2,1)} collective-permute-done((bf16[64,4000]{1,0:T(8,128)(2,1)}, bf16[64,4000]{1,0:T(8,128)(2,1)}, u32[]{:S(2)}, u32[]{:S(2)}) %collective-permute-start) | collective-permute-done | bytes 512032 | tf_op jit(solution)/shard_map/ppermute | solution.py:15
  19.5 0.0 collective-permute-start.2
  19.6 0.0 collective-permute-done.1
  19.6 5.3 %collective-permute-start.3 = (bf16[64,4000]{1,0:T(8,128)(2,1)S(1)}, bf16[64,4000]{1,0:T(8,128)(2,1)S(1)}, u32[]{:S(2)}, u32[]{:S(2)}) collective-permute-start(bf16[64,4000]{1,0:T(8,128)(2,1)S(1)} %collective-permute-done.1), channel_id=1, source_target_pairs={{0,120},{8,0},{16,8},{24,16},{32,24},{40,32},{48,40},{56,48},{64,5... | collective-permute-start | bytes 1536008 | tf_op jit(solution)/shard_map/ppermute | solution.py:18
  24.9 1.1 constant_dynamic-update-slice_fusion.14
  26.0 10.1 %collective-permute-done.2 = bf16[64,4000]{1,0:T(8,128)(2,1)S(1)} collective-permute-done((bf16[64,4000]{1,0:T(8,128)(2,1)}, bf16[64,4000]{1,0:T(8,128)(2,1)S(1)}, u32[]{:S(2)}, u32[]{:S(2)}) %collective-permute-start.2) | collective-permute-done | bytes 512032 | tf_op jit(solution)/shard_map/ppermute | solution.py:15
  36.2 0.0 collective-permute-start.4
  36.2 0.0 collective-permute-done.3
  36.2 5.3 %collective-permute-start.5 = (bf16[64,4000]{1,0:T(8,128)(2,1)S(1)}, bf16[64,4000]{1,0:T(8,128)(2,1)S(1)}, u32[]{:S(2)}, u32[]{:S(2)}) collective-permute-start(bf16[64,4000]{1,0:T(8,128)(2,1)S(1)} %collective-permute-done.3), channel_id=1, source_target_pairs={{0,120},{8,0},{16,8},{24,16},{32,24},{40,32},{48,40},{56,48},{64,5... | collective-permute-start | bytes 1536008 | tf_op jit(solution)/shard_map/ppermute | solution.py:18
  41.6 10.1 %collective-permute-done.4 = bf16[64,4000]{1,0:T(8,128)(2,1)S(1)} collective-permute-done((bf16[64,4000]{1,0:T(8,128)(2,1)S(1)}, bf16[64,4000]{1,0:T(8,128)(2,1)S(1)}, u32[]{:S(2)}, u32[]{:S(2)}) %collective-permute-start.4) | collective-permute-done | bytes 512032 | tf_op jit(solution)/shard_map/ppermute | solution.py:15
  51.7 0.0 collective-permute-start.6
  51.7 0.0 collective-permute-done.5
  51.7 5.3 %collective-permute-start.7 = (bf16[64,4000]{1,0:T(8,128)(2,1)S(1)}, bf16[64,4000]{1,0:T(8,128)(2,1)S(1)}, u32[]{:S(2)}, u32[]{:S(2)}) collective-permute-start(bf16[64,4000]{1,0:T(8,128)(2,1)S(1)} %collective-permute-done.5), channel_id=1, source_target_pairs={{0,120},{8,0},{16,8},{24,16},{32,24},{40,32},{48,40},{56,48},{64,5... | collective-permute-start | bytes 1536008 | tf_op jit(solution)/shard_map/ppermute | solution.py:18
  57.2 9.3 %collective-permute-done.6 = bf16[64,4000]{1,0:T(8,128)(2,1)S(1)} collective-permute-done((bf16[64,4000]{1,0:T(8,128)(2,1)S(1)}, bf16[64,4000]{1,0:T(8,128)(2,1)S(1)}, u32[]{:S(2)}, u32[]{:S(2)}) %collective-permute-start.6) | collective-permute-done | bytes 512032 | tf_op jit(solution)/shard_map/ppermute | solution.py:15
  66.4 0.0 collective-permute-start.8
  66.4 0.0 collective-permute-done.7
  66.4 5.3 %collective-permute-start.9 = (bf16[64,4000]{1,0:T(8,128)(2,1)S(1)}, bf16[64,4000]{1,0:T(8,128)(2,1)S(1)}, u32[]{:S(2)}, u32[]{:S(2)}) collective-permute-start(bf16[64,4000]{1,0:T(8,128)(2,1)S(1)} %collective-permute-done.7), channel_id=1, source_target_pairs={{0,120},{8,0},{16,8},{24,16},{32,24},{40,32},{48,40},{56,48},{64,5... | collective-permute-start | bytes 1536008 | tf_op jit(solution)/shard_map/ppermute | solution.py:18
  71.9 8.4 %collective-permute-done.8 = bf16[64,4000]{1,0:T(8,128)(2,1)S(1)} collective-permute-done((bf16[64,4000]{1,0:T(8,128)(2,1)S(1)}, bf16[64,4000]{1,0:T(8,128)(2,1)S(1)}, u32[]{:S(2)}, u32[]{:S(2)}) %collective-permute-start.8) | collective-permute-done | bytes 512032 | tf_op jit(solution)/shard_map/ppermute | solution.py:15
  80.3 0.0 collective-permute-start.10
  80.3 0.0 collective-permute-done.9
  80.3 5.3 %collective-permute-start.11 = (bf16[64,4000]{1,0:T(8,128)(2,1)S(1)}, bf16[64,4000]{1,0:T(8,128)(2,1)S(1)}, u32[]{:S(2)}, u32[]{:S(2)}) collective-permute-start(bf16[64,4000]{1,0:T(8,128)(2,1)S(1)} %collective-permute-done.9), channel_id=1, source_target_pairs={{0,120},{8,0},{16,8},{24,16},{32,24},{40,32},{48,40},{56,48},{64,5... | collective-permute-start | bytes 1536008 | tf_op jit(solution)/shard_map/ppermute | solution.py:18
  85.7 7.5 %collective-permute-done.10 = bf16[64,4000]{1,0:T(8,128)(2,1)S(1)} collective-permute-done((bf16[64,4000]{1,0:T(8,128)(2,1)S(1)}, bf16[64,4000]{1,0:T(8,128)(2,1)S(1)}, u32[]{:S(2)}, u32[]{:S(2)}) %collective-permute-start.10) | collective-permute-done | bytes 512032 | tf_op jit(solution)/shard_map/ppermute | solution.py:15
  93.2 0.0 collective-permute-start.12
  93.2 0.0 collective-permute-done.11
  93.3 5.3 %collective-permute-start.13 = (bf16[64,4000]{1,0:T(8,128)(2,1)S(1)}, bf16[64,4000]{1,0:T(8,128)(2,1)S(1)}, u32[]{:S(2)}, u32[]{:S(2)}) collective-permute-start(bf16[64,4000]{1,0:T(8,128)(2,1)S(1)} %collective-permute-done.11), channel_id=1, source_target_pairs={{0,120},{8,0},{16,8},{24,16},{32,24},{40,32},{48,40},{56,48},{64,5... | collective-permute-start | bytes 1536008 | tf_op jit(solution)/shard_map/ppermute | solution.py:18
  98.7 7.3 %collective-permute-done.12 = bf16[64,4000]{1,0:T(8,128)(2,1)S(1)} collective-permute-done((bf16[64,4000]{1,0:T(8,128)(2,1)S(1)}, bf16[64,4000]{1,0:T(8,128)(2,1)S(1)}, u32[]{:S(2)}, u32[]{:S(2)}) %collective-permute-start.12) | collective-permute-done | bytes 512032 | tf_op jit(solution)/shard_map/ppermute | solution.py:15
  106.0 0.0 collective-permute-start.14
  106.0 0.0 collective-permute-done.13
  106.1 12.4 %collective-permute-done.14 = bf16[64,4000]{1,0:T(8,128)(2,1)S(1)} collective-permute-done((bf16[64,4000]{1,0:T(8,128)(2,1)S(1)}, bf16[64,4000]{1,0:T(8,128)(2,1)S(1)}, u32[]{:S(2)}, u32[]{:S(2)}) %collective-permute-start.14) | collective-permute-done | bytes 512032 | tf_op jit(solution)/shard_map/ppermute | solution.py:15
  118.5 4.5 %fusion.31 = (f32[512]{0:T(512)S(1)}, f32[512,4000]{0,1:T(8,128)S(1)}) fusion(bf16[1024,4000]{1,0:T(8,128)(2,1)S(1)} %constant_dynamic-update-slice_fusion, bf16[1024,1024]{1,0:T(8,128)(2,1)S(1)} %fusion.3), kind=kOutput, calls=%fused_computation.70 | convolution fusion | flops 4196351488 | bytes 17631232 | tf_op jit(solution)/shard_map/dot_general | solution.py:41
  123.0 9.2 %fusion.32 = (f32[512]{0:T(512)S(1)}, f32[512,4000]{0,1:T(8,128)}) fusion(bf16[1024,4000]{1,0:T(8,128)(2,1)S(1)} %constant_dynamic-update-slice_fusion, bf16[1024,1024]{1,0:T(8,128)(2,1)S(1)} %fusion.3), kind=kOutput, calls=%fused_computation.71 | convolution fusion | flops 4196351488 | bytes 17631232 | tf_op jit(solution)/shard_map/dot_general | solution.py:41
  132.2 7.8 %exponential_reduce_fusion.1 = (f32[512]{0:T(512)S(1)}, f32[512]{0:T(512)S(1)}, f32[512]{0:T(512)S(1)}, f32[512]{0:T(512)S(1)}, f32[512]{0:T(512)S(1)}, /*index=5*/f32[512]{0:T(512)S(1)}) fusion(f32[512,4000]{0,1:T(8,128)S(1)} %get-tuple-element.32, f32[512]{0:T(512)S(1)} %get-tuple-element.31, s32[512]{0:T(512)S(1)} %bitcast.63, s32[4000]{0:T(1024)S(1)} %iota_add_fusion, ...), kind=kLoop, calls=%fused_computation.3 | loop fusion | flops 28668928 | bytes 16420480 | tf_op jit(solution)/shard_map/reduce_sum | solution.py:45
  140.0 0.7 broadcast_in_dim.17
  140.7 4.3 %all-to-all-start = ((f32[8,4,1024]{2,1,0:T(4,128)}), f32[8,4,1024]{2,1,0:T(4,128)S(1)}, u32[]{:S(2)}, u32[]{:S(2)}) async-start(f32[8,4,1024]{2,1,0:T(4,128)} %broadcast_in_dim.17), calls=%async_computation | async-start | bytes 262144 | tf_op jit(solution)/shard_map/all_to_all | solution.py:57
  145.0 6.1 %all-to-all-done = f32[8,4,1024]{2,1,0:T(4,128)S(1)} async-done(((f32[8,4,1024]{2,1,0:T(4,128)}), f32[8,4,1024]{2,1,0:T(4,128)S(1)}, u32[]{:S(2)}, u32[]{:S(2)}) %all-to-all-start) | async-done | bytes 131104 | tf_op jit(solution)/shard_map/all_to_all | solution.py:57
  151.1 0.1 fusion.29
  151.3 0.8 fusion.27
  152.1 0.2 fusion.13
  152.3 10.1 %all_to_all.10 = f32[16,4,3]{1,2,0:T(4,128)S(1)} all-to-all(f32[16,4,3]{1,2,0:T(4,128)S(1)} %broadcast_in_dim.19), channel_id=1, replica_groups=mesh['dp'=16,'vocab'=8] {'dp'}, dimensions={0} | all-to-all | bytes 1536 | tf_op jit(solution)/shard_map/all_to_all | solution.py:79
  162.5 0.6 pad_maximum_fusion
  (34 shorter events, 0.8 us)
Async XLA Ops:
  0.6 13.1 %copy-start = (bf16[64,4000]{1,0:T(8,128)(2,1)S(1)}, bf16[64,4000]{1,0:T(8,128)(2,1)}, u32[]{:S(2)}) copy-start(bf16[64,4000]{1,0:T(8,128)(2,1)} %param.9) | copy-start | bytes 1536004
  0.6 18.9 %collective-permute-start = (bf16[64,4000]{1,0:T(8,128)(2,1)}, bf16[64,4000]{1,0:T(8,128)(2,1)}, u32[]{:S(2)}, u32[]{:S(2)}) collective-permute-start(bf16[64,4000]{1,0:T(8,128)(2,1)} %param.9), channel_id=1, source_target_pairs={{0,8},{8,16},{16,24},{24,32},{32,40},{40,48},{48,56},{56,64},{64,7... | collective-permute-start | bytes 1536008 | tf_op jit(solution)/shard_map/ppermute | solution.py:15
  2.4 17.2 %collective-permute-start.1 = (bf16[64,4000]{1,0:T(8,128)(2,1)}, bf16[64,4000]{1,0:T(8,128)(2,1)S(1)}, u32[]{:S(2)}, u32[]{:S(2)}) collective-permute-start(bf16[64,4000]{1,0:T(8,128)(2,1)} %param.9), channel_id=1, source_target_pairs={{0,120},{8,0},{16,8},{24,16},{32,24},{40,32},{48,40},{56,48},{64,5... | collective-permute-start | bytes 1536008 | tf_op jit(solution)/shard_map/ppermute | solution.py:18
  19.5 16.6 %collective-permute-start.2 = (bf16[64,4000]{1,0:T(8,128)(2,1)}, bf16[64,4000]{1,0:T(8,128)(2,1)S(1)}, u32[]{:S(2)}, u32[]{:S(2)}) collective-permute-start(bf16[64,4000]{1,0:T(8,128)(2,1)} %collective-permute-done), channel_id=1, source_target_pairs={{0,8},{8,16},{16,24},{24,32},{32,40},{40,48},{48,56},{56,64},{64,7... | collective-permute-start | bytes 1536008 | tf_op jit(solution)/shard_map/ppermute | solution.py:15
  19.6 16.6 %collective-permute-start.3 = (bf16[64,4000]{1,0:T(8,128)(2,1)S(1)}, bf16[64,4000]{1,0:T(8,128)(2,1)S(1)}, u32[]{:S(2)}, u32[]{:S(2)}) collective-permute-start(bf16[64,4000]{1,0:T(8,128)(2,1)S(1)} %collective-permute-done.1), channel_id=1, source_target_pairs={{0,120},{8,0},{16,8},{24,16},{32,24},{40,32},{48,40},{56,48},{64,5... | collective-permute-start | bytes 1536008 | tf_op jit(solution)/shard_map/ppermute | solution.py:18
  36.2 15.6 %collective-permute-start.4 = (bf16[64,4000]{1,0:T(8,128)(2,1)S(1)}, bf16[64,4000]{1,0:T(8,128)(2,1)S(1)}, u32[]{:S(2)}, u32[]{:S(2)}) collective-permute-start(bf16[64,4000]{1,0:T(8,128)(2,1)S(1)} %collective-permute-done.2), channel_id=1, source_target_pairs={{0,8},{8,16},{16,24},{24,32},{32,40},{40,48},{48,56},{56,64},{64,7... | collective-permute-start | bytes 1536008 | tf_op jit(solution)/shard_map/ppermute | solution.py:15
  36.2 15.6 %collective-permute-start.5 = (bf16[64,4000]{1,0:T(8,128)(2,1)S(1)}, bf16[64,4000]{1,0:T(8,128)(2,1)S(1)}, u32[]{:S(2)}, u32[]{:S(2)}) collective-permute-start(bf16[64,4000]{1,0:T(8,128)(2,1)S(1)} %collective-permute-done.3), channel_id=1, source_target_pairs={{0,120},{8,0},{16,8},{24,16},{32,24},{40,32},{48,40},{56,48},{64,5... | collective-permute-start | bytes 1536008 | tf_op jit(solution)/shard_map/ppermute | solution.py:18
  51.7 14.7 %collective-permute-start.6 = (bf16[64,4000]{1,0:T(8,128)(2,1)S(1)}, bf16[64,4000]{1,0:T(8,128)(2,1)S(1)}, u32[]{:S(2)}, u32[]{:S(2)}) collective-permute-start(bf16[64,4000]{1,0:T(8,128)(2,1)S(1)} %collective-permute-done.4), channel_id=1, source_target_pairs={{0,8},{8,16},{16,24},{24,32},{32,40},{40,48},{48,56},{56,64},{64,7... | collective-permute-start | bytes 1536008 | tf_op jit(solution)/shard_map/ppermute | solution.py:15
  51.7 14.7 %collective-permute-start.7 = (bf16[64,4000]{1,0:T(8,128)(2,1)S(1)}, bf16[64,4000]{1,0:T(8,128)(2,1)S(1)}, u32[]{:S(2)}, u32[]{:S(2)}) collective-permute-start(bf16[64,4000]{1,0:T(8,128)(2,1)S(1)} %collective-permute-done.5), channel_id=1, source_target_pairs={{0,120},{8,0},{16,8},{24,16},{32,24},{40,32},{48,40},{56,48},{64,5... | collective-permute-start | bytes 1536008 | tf_op jit(solution)/shard_map/ppermute | solution.py:18
  66.4 13.8 %collective-permute-start.8 = (bf16[64,4000]{1,0:T(8,128)(2,1)S(1)}, bf16[64,4000]{1,0:T(8,128)(2,1)S(1)}, u32[]{:S(2)}, u32[]{:S(2)}) collective-permute-start(bf16[64,4000]{1,0:T(8,128)(2,1)S(1)} %collective-permute-done.6), channel_id=1, source_target_pairs={{0,8},{8,16},{16,24},{24,32},{32,40},{40,48},{48,56},{56,64},{64,7... | collective-permute-start | bytes 1536008 | tf_op jit(solution)/shard_map/ppermute | solution.py:15
  66.4 13.8 %collective-permute-start.9 = (bf16[64,4000]{1,0:T(8,128)(2,1)S(1)}, bf16[64,4000]{1,0:T(8,128)(2,1)S(1)}, u32[]{:S(2)}, u32[]{:S(2)}) collective-permute-start(bf16[64,4000]{1,0:T(8,128)(2,1)S(1)} %collective-permute-done.7), channel_id=1, source_target_pairs={{0,120},{8,0},{16,8},{24,16},{32,24},{40,32},{48,40},{56,48},{64,5... | collective-permute-start | bytes 1536008 | tf_op jit(solution)/shard_map/ppermute | solution.py:18
  80.3 13.0 %collective-permute-start.10 = (bf16[64,4000]{1,0:T(8,128)(2,1)S(1)}, bf16[64,4000]{1,0:T(8,128)(2,1)S(1)}, u32[]{:S(2)}, u32[]{:S(2)}) collective-permute-start(bf16[64,4000]{1,0:T(8,128)(2,1)S(1)} %collective-permute-done.8), channel_id=1, source_target_pairs={{0,8},{8,16},{16,24},{24,32},{32,40},{40,48},{48,56},{56,64},{64,7... | collective-permute-start | bytes 1536008 | tf_op jit(solution)/shard_map/ppermute | solution.py:15
  80.3 13.0 %collective-permute-start.11 = (bf16[64,4000]{1,0:T(8,128)(2,1)S(1)}, bf16[64,4000]{1,0:T(8,128)(2,1)S(1)}, u32[]{:S(2)}, u32[]{:S(2)}) collective-permute-start(bf16[64,4000]{1,0:T(8,128)(2,1)S(1)} %collective-permute-done.9), channel_id=1, source_target_pairs={{0,120},{8,0},{16,8},{24,16},{32,24},{40,32},{48,40},{56,48},{64,5... | collective-permute-start | bytes 1536008 | tf_op jit(solution)/shard_map/ppermute | solution.py:18
  93.2 12.8 %collective-permute-start.12 = (bf16[64,4000]{1,0:T(8,128)(2,1)S(1)}, bf16[64,4000]{1,0:T(8,128)(2,1)S(1)}, u32[]{:S(2)}, u32[]{:S(2)}) collective-permute-start(bf16[64,4000]{1,0:T(8,128)(2,1)S(1)} %collective-permute-done.10), channel_id=1, source_target_pairs={{0,8},{8,16},{16,24},{24,32},{32,40},{40,48},{48,56},{56,64},{64,7... | collective-permute-start | bytes 1536008 | tf_op jit(solution)/shard_map/ppermute | solution.py:15
  93.3 12.8 %collective-permute-start.13 = (bf16[64,4000]{1,0:T(8,128)(2,1)S(1)}, bf16[64,4000]{1,0:T(8,128)(2,1)S(1)}, u32[]{:S(2)}, u32[]{:S(2)}) collective-permute-start(bf16[64,4000]{1,0:T(8,128)(2,1)S(1)} %collective-permute-done.11), channel_id=1, source_target_pairs={{0,120},{8,0},{16,8},{24,16},{32,24},{40,32},{48,40},{56,48},{64,5... | collective-permute-start | bytes 1536008 | tf_op jit(solution)/shard_map/ppermute | solution.py:18
  106.0 12.5 %collective-permute-start.14 = (bf16[64,4000]{1,0:T(8,128)(2,1)S(1)}, bf16[64,4000]{1,0:T(8,128)(2,1)S(1)}, u32[]{:S(2)}, u32[]{:S(2)}) collective-permute-start(bf16[64,4000]{1,0:T(8,128)(2,1)S(1)} %collective-permute-done.12), channel_id=1, source_target_pairs={{0,8},{8,16},{16,24},{24,32},{32,40},{40,48},{48,56},{56,64},{64,7... | collective-permute-start | bytes 1536008 | tf_op jit(solution)/shard_map/ppermute | solution.py:15
  132.2 12.8 %copy-start.1 = (s32[2]{0:T(128)S(1)}, s32[2]{0:T(128)}, u32[]{:S(2)}) copy-start(s32[2]{0:T(128)} %param.11) | copy-start | bytes 28
  132.2 19.9 %copy-start.3 = (s32[2,1]{0,1:T(1,128)S(1)}, s32[2,1]{0,1:T(1,128)}, u32[]{:S(2)}) copy-start(s32[2,1]{0,1:T(1,128)} %param.12) | copy-start | bytes 28
  132.2 30.3 %copy-start.2 = (f32[4]{0:T(128)S(1)}, f32[4]{0:T(128)}, u32[]{:S(2)}) copy-start(f32[4]{0:T(128)} %param.13) | copy-start | bytes 52
  140.7 10.4 %all-to-all-start = ((f32[8,4,1024]{2,1,0:T(4,128)}), f32[8,4,1024]{2,1,0:T(4,128)S(1)}, u32[]{:S(2)}, u32[]{:S(2)}) async-start(f32[8,4,1024]{2,1,0:T(4,128)} %broadcast_in_dim.17), calls=%async_computation | async-start | bytes 262144 | tf_op jit(solution)/shard_map/all_to_all | solution.py:57
